TPU v7x, 32 devices: a whole 2x2x4 slice. The times are simulated.
32 devices in a mesh: img: 8 (over z, core), slab: 4 (over y, x).
Axes of the slice: x: 2, y: 2, z: 4, core: 2. Of those that a mesh axis runs over, the one named last changes fastest.
Arguments:
- image_masses: float32 [8, 3072, 3072], P('img', 'slab'), may hold values from 0.1 to 10
- dual_multipliers: float32 [8, 3072, 3072], P('img', 'slab'), may hold values from 0.1 to 10
- fraction_tops: int32 [8], P('img'), may hold values from 1 to 8
- banded_submatrices: bfloat16 [24, 3, 128, 128], replicated, as said below
- band_starts: int32 [24, 3], replicated, may hold values from -2 to 2, as said below
Outputs:
- barycenter: float32 [3072, 3072], P('slab')
- new_scalings: float32 [8, 3072, 3072], P('img', 'slab')
Inputs may be any that keep to these rules, and one draw needn't show every extreme that they name: `band_starts`: each row of offsets holds three consecutive numbers in increasing order; the first row is 0, 1, 2 and the last row is -2, -1, 0. `banded_submatrices`: all entries are positive.
All inputs are finite; a program needn't handle non-finite values.
Results may differ from a plain program's by a relative error of at most 0.0032.
Values may be sent and summed in bfloat16 or wider, within the bound.
No kernel may reach another device: no remote copies, remote signals or barrier semaphores. Data moves between devices by JAX's collectives and lax.ppermute only.
A program may use at most 192 MiB of HBM per device.

v0:
```python
import jax
import jax.numpy as jnp
from jax import lax
from jax.sharding import PartitionSpec as P

ITERS = 2


def offset_terms(banded_submatrices, band_starts):
    offsets = jnp.arange(-2, 3, dtype=jnp.int32)
    matches = band_starts[:, None, :] == offsets[None, :, None]
    picked = jnp.where(
        matches[:, :, :, None, None], banded_submatrices[:, None], jnp.zeros((), jnp.bfloat16)
    )
    return jnp.sum(picked, axis=2)


def column_sweep(field, terms):
    block_stack = terms.shape[0]
    width = terms.shape[2]
    count = field.shape[0]
    height = field.shape[1]
    leading = field.reshape((count * height, block_stack, width)).transpose(1, 0, 2)
    padded = jnp.pad(leading, ((2, 2), (0, 0), (0, 0)))
    total = jnp.zeros((block_stack, count * height, width), jnp.float32)
    for offset in range(5):
        total = total + lax.dot_general(
            padded[offset : offset + block_stack],
            terms[:, offset],
            (((2,), (2,)), ((0,), (0,))),
            preferred_element_type=jnp.float32,
        )
    return total.transpose(1, 0, 2).reshape((count, height, block_stack * width))


def rows_pass(padded, terms):
    block_stack = terms.shape[0]
    width = terms.shape[2]
    columns = padded.shape[2]
    split = padded[0].reshape((block_stack + 4, width, columns))
    total = jnp.zeros((block_stack, width, columns), jnp.float32)
    for offset in range(5):
        total = total + lax.dot_general(
            terms[:, offset],
            split[offset : offset + block_stack],
            (((2,), (1,)), ((0,), (0,))),
            preferred_element_type=jnp.float32,
        )
    outputs = [total.reshape((block_stack * width, columns))]
    return jnp.stack(outputs, axis=0)


def per_device(image_masses, dual_multipliers, fraction_tops, banded_submatrices, band_starts):
    width = banded_submatrices.shape[2]
    terms = offset_terms(banded_submatrices, band_starts)
    total_weight = lax.psum(jnp.sum(fraction_tops).astype(jnp.float32), "img")
    weights = fraction_tops.astype(jnp.float32)

    def apply_kernel(field):
        inner = column_sweep(field, terms).astype(jnp.bfloat16)
        columns = lax.all_to_all(inner, "slab", split_axis=2, concat_axis=1, tiled=True)
        padded = jnp.pad(columns, ((0, 0), (2 * width, 2 * width), (0, 0)))
        result = rows_pass(padded, terms).astype(jnp.bfloat16)
        return lax.all_to_all(result, "slab", split_axis=1, concat_axis=2, tiled=True)

    latest_multiplier = dual_multipliers
    barycenter = jnp.zeros(image_masses.shape[1:], jnp.float32)
    for iteration in range(ITERS):
        kernel_v = apply_kernel(latest_multiplier.astype(jnp.bfloat16))
        scaled_u = (image_masses / kernel_v.astype(jnp.float32)).astype(jnp.bfloat16)
        kernel_u = apply_kernel(scaled_u)
        value_portion = jnp.einsum("i,irc->rc", weights, jnp.log(kernel_u.astype(jnp.float32)))
        barycenter = jnp.exp(lax.psum(value_portion, "img") / total_weight)
        latest_multiplier = barycenter[None] / kernel_u.astype(jnp.float32)
    return (barycenter, latest_multiplier)


def solution(mesh):
    placed = (P("img", "slab", None), P("img", "slab", None), P("img"), P(), P())
    return jax.shard_map(
        per_device,
        mesh=mesh,
        in_specs=placed,
        out_specs=(P("slab", None), P("img", "slab", None)),
        check_vma=False,
    )
```

profile of v0, /device:TPU:0, one launch (start us, length us, event | category | flops | bytes accessed | tf_op | source)
XLA Modules:
  0.0 2068.6 jit_solution(6369687439953317268)
XLA Ops:
  77.7 49.0 %reduce.1 = bf16[3072,768]{1,0:T(8,128)(2,1)} reduce(bf16[3072,1,768]{2,1,0:T(2,128)(2,1)} %bitcast.287, bf16[]{:T(256)} %broadcast.49), dimensions={1}, to_apply=%bitcast.273.reduce_sub_computation | reduce | bytes 9437186
  132.1 61.0 %all_to_all.108 = bf16[4,2,294912]{2,1,0:T(2,128)(2,1)} all-to-all(bf16[4,2,294912]{2,1,0:T(2,128)(2,1)} %reshape.244), channel_id=1, replica_groups=mesh['img'=8,'slab'=4] {'slab'}, dimensions={0} | all-to-all | bytes 9437184 | tf_op jit(solution)/shard_map/all_to_all | solution.py:61
  269.0 49.2 %reduce.2 = bf16[3072,768]{1,0:T(8,128)(2,1)} reduce(bf16[3072,1,768]{2,1,0:T(2,128)(2,1)} %bitcast.290, bf16[]{:T(256)} %broadcast.49), dimensions={1}, to_apply=%bitcast.272.reduce_sub_computation | reduce | bytes 9437186
  338.2 42.8 %all-to-all-done.1 = bf16[4,2,294912]{2,1,0:T(2,128)(2,1)} async-done(((bf16[4,2,294912]{2,1,0:T(2,128)(2,1)}), bf16[4,2,294912]{2,1,0:T(2,128)(2,1)}, u32[]{:S(2)}, u32[]{:S(2)}) %all-to-all-start.1) | async-done | bytes 4718624 | tf_op jit(solution)/shard_map/all_to_all | solution.py:64
  389.0 23.5 %copy.138 = f32[1,4,768,768]{2,3,1,0:T(8,128)} copy(bf16[1,4,768,768]{3,0,2,1:T(2,128)(2,1)} %bitcast.291) | data formatting | bytes 14155776 | tf_op jit(solution)/shard_map/convert_element_type | solution.py:70
  478.4 49.4 %reduce.3 = bf16[3072,768]{1,0:T(8,128)(2,1)} reduce(bf16[3072,1,768]{2,1,0:T(2,128)(2,1)} %bitcast.292, bf16[]{:T(256)} %broadcast.49), dimensions={1}, to_apply=%bitcast.271.reduce_sub_computation | reduce | bytes 9437186
  533.1 58.9 %all_to_all.109 = bf16[4,2,294912]{2,1,0:T(2,128)(2,1)} all-to-all(bf16[4,2,294912]{2,1,0:T(2,128)(2,1)} %reshape.248), channel_id=1, replica_groups=mesh['img'=8,'slab'=4] {'slab'}, dimensions={0} | all-to-all | bytes 9437184 | tf_op jit(solution)/shard_map/all_to_all | solution.py:61
  667.7 49.1 %reduce.4 = bf16[3072,768]{1,0:T(8,128)(2,1)} reduce(bf16[3072,1,768]{2,1,0:T(2,128)(2,1)} %bitcast.294, bf16[]{:T(256)} %broadcast.49), dimensions={1}, to_apply=%bitcast.270.reduce_sub_computation | reduce | bytes 9437186
  727.9 50.3 %all-to-all-done.3 = bf16[4,2,294912]{2,1,0:T(2,128)(2,1)} async-done(((bf16[4,2,294912]{2,1,0:T(2,128)(2,1)}), bf16[4,2,294912]{2,1,0:T(2,128)(2,1)}, u32[]{:S(2)}, u32[]{:S(2)}) %all-to-all-start.3) | async-done | bytes 4718624 | tf_op jit(solution)/shard_map/all_to_all | solution.py:64
  801.7 23.3 %copy.145 = f32[1,4,768,768]{2,3,1,0:T(8,128)} copy(f32[1,4,768,768]{3,0,2,1:T(1,128)} %bitcast.302) | data formatting | bytes 18874368 | tf_op jit(solution)/shard_map/i,irc->rc/dot_general | solution.py:72
  841.9 23.6 %copy.146 = f32[1,4,768,768]{2,3,1,0:T(8,128)} copy(bf16[1,4,768,768]{3,0,2,1:T(2,128)(2,1)} %bitcast.274) | data formatting | bytes 14155776 | tf_op jit(solution)/shard_map/convert_element_type | solution.py:72
  865.5 155.0 %all-reduce.11.cloned.1.call-done = f32[768,3072]{0,1:T(8,128)} async-done(((f32[768,3072]{0,1:T(8,128)}), f32[768,3072]{0,1:T(8,128)}) %all-reduce.11.cloned.1.call-update) | async-done | bytes 9437200 | tf_op jit(solution)/shard_map/psum | solution.py:73
  1086.8 49.4 %reduce.5 = bf16[3072,768]{1,0:T(8,128)(2,1)} reduce(bf16[3072,1,768]{2,1,0:T(2,128)(2,1)} %bitcast.295, bf16[]{:T(256)} %broadcast.49), dimensions={1}, to_apply=%bitcast.269.reduce_sub_computation | reduce | bytes 9437186
  1141.6 59.5 %all_to_all.110 = bf16[4,2,294912]{2,1,0:T(2,128)(2,1)} all-to-all(bf16[4,2,294912]{2,1,0:T(2,128)(2,1)} %reshape.252), channel_id=1, replica_groups=mesh['img'=8,'slab'=4] {'slab'}, dimensions={0} | all-to-all | bytes 9437184 | tf_op jit(solution)/shard_map/all_to_all | solution.py:61
  1276.9 49.1 %reduce.6 = bf16[3072,768]{1,0:T(8,128)(2,1)} reduce(bf16[3072,1,768]{2,1,0:T(2,128)(2,1)} %bitcast.297, bf16[]{:T(256)} %broadcast.49), dimensions={1}, to_apply=%bitcast.268.reduce_sub_computation | reduce | bytes 9437186
  1331.4 58.2 %all_to_all.111 = bf16[4,2,294912]{2,1,0:T(2,128)(2,1)} all-to-all(bf16[4,2,294912]{2,1,0:T(2,128)(2,1)} %reshape.254), channel_id=1, replica_groups=mesh['img'=8,'slab'=4] {'slab'}, dimensions={0} | all-to-all | bytes 9437184 | tf_op jit(solution)/shard_map/all_to_all | solution.py:64
  1397.6 23.5 %copy.152 = f32[1,4,768,768]{2,3,1,0:T(8,128)} copy(bf16[1,4,768,768]{3,0,2,1:T(2,128)(2,1)} %bitcast.298) | data formatting | bytes 14155776 | tf_op jit(solution)/shard_map/convert_element_type | solution.py:70
  1486.9 49.4 %reduce.7 = bf16[3072,768]{1,0:T(8,128)(2,1)} reduce(bf16[3072,1,768]{2,1,0:T(2,128)(2,1)} %bitcast.299, bf16[]{:T(256)} %broadcast.49), dimensions={1}, to_apply=%bitcast.267.reduce_sub_computation | reduce | bytes 9437186
  1541.8 56.8 %all_to_all.112 = bf16[4,2,294912]{2,1,0:T(2,128)(2,1)} all-to-all(bf16[4,2,294912]{2,1,0:T(2,128)(2,1)} %reshape.256), channel_id=1, replica_groups=mesh['img'=8,'slab'=4] {'slab'}, dimensions={0} | all-to-all | bytes 9437184 | tf_op jit(solution)/shard_map/all_to_all | solution.py:61
  1674.4 49.2 %reduce.8 = bf16[3072,768]{1,0:T(8,128)(2,1)} reduce(bf16[3072,1,768]{2,1,0:T(2,128)(2,1)} %bitcast.288, bf16[]{:T(256)} %broadcast.49), dimensions={1}, to_apply=%bitcast.266.reduce_sub_computation | reduce | bytes 9437186
  1729.0 55.4 %all_to_all.113 = bf16[4,2,294912]{2,1,0:T(2,128)(2,1)} all-to-all(bf16[4,2,294912]{2,1,0:T(2,128)(2,1)} %reshape.258), channel_id=1, replica_groups=mesh['img'=8,'slab'=4] {'slab'}, dimensions={0} | all-to-all | bytes 9437184 | tf_op jit(solution)/shard_map/all_to_all | solution.py:64
  1807.7 23.3 %copy.159 = f32[1,4,768,768]{2,3,1,0:T(8,128)} copy(f32[1,4,768,768]{3,0,2,1:T(1,128)} %bitcast.301) | data formatting | bytes 18874368 | tf_op jit(solution)/shard_map/i,irc->rc/dot_general | solution.py:72
  1831.0 23.5 %copy.160 = f32[1,4,768,768]{2,3,1,0:T(8,128)} copy(bf16[1,4,768,768]{3,0,2,1:T(2,128)(2,1)} %bitcast.275) | data formatting | bytes 14155776 | tf_op jit(solution)/shard_map/convert_element_type | solution.py:72
  1854.5 172.9 %all-reduce.13.cloned.1.call-done = f32[768,3072]{0,1:T(8,128)} async-done(((f32[768,3072]{0,1:T(8,128)}), f32[768,3072]{0,1:T(8,128)}) %all-reduce.13.cloned.1.call-update) | async-done | bytes 9437200 | tf_op jit(solution)/shard_map/psum | solution.py:73
  (136 shorter events, 748.3 us)
Async XLA Ops:
  15.6 6.9 copy-start.16
  26.3 18.9 copy-start
  26.3 8.9 copy-start.12
  214.4 7.8 copy-start.8
  222.3 3.8 copy-start.1
  323.6 57.3 %all-to-all-start.1 = ((bf16[4,2,294912]{2,1,0:T(2,128)(2,1)}), bf16[4,2,294912]{2,1,0:T(2,128)(2,1)}, u32[]{:S(2)}, u32[]{:S(2)}) async-start(bf16[4,2,294912]{2,1,0:T(2,128)(2,1)} %reshape.246), calls=%async_computation.1 | async-start | bytes 9437184 | tf_op jit(solution)/shard_map/all_to_all | solution.py:64
  429.2 7.7 copy-start.2
  429.2 7.7 copy-start.13
  613.3 7.7 copy-start.9
  621.0 3.8 copy-start.3
  722.3 56.0 %all-to-all-start.3 = ((bf16[4,2,294912]{2,1,0:T(2,128)(2,1)}), bf16[4,2,294912]{2,1,0:T(2,128)(2,1)}, u32[]{:S(2)}, u32[]{:S(2)}) async-start(bf16[4,2,294912]{2,1,0:T(2,128)(2,1)} %reshape.250), calls=%async_computation.3 | async-start | bytes 9437184 | tf_op jit(solution)/shard_map/all_to_all | solution.py:64
  727.2 293.3 %all-reduce.11.cloned.1.call-start = ((), (), s32[]{:S(2)}) async-start(), calls=%async_computation.8 | async-start | bytes 18874368 | tf_op jit(solution)/shard_map/psum | solution.py:73
  824.9 1202.4 %all-reduce.13.cloned.1.call-start = ((), (), s32[]{:S(2)}) async-start(), calls=%async_computation.9 | async-start | bytes 18874368 | tf_op jit(solution)/shard_map/psum | solution.py:73
  1037.6 7.7 copy-start.4
  1037.6 7.7 copy-start.14
  1222.4 7.7 copy-start.10
  1230.1 3.8 copy-start.5
  1437.7 7.8 copy-start.6
  1437.7 7.8 copy-start.15
  1619.9 7.8 copy-start.11
  1627.7 3.8 copy-start.7
Sparse Core Ops, SparseCore 0:
  825.1 195.3 all-reduce.10
  1831.1 196.2 all-reduce.12
where the time goes:
time: 2080 us; the launch traced here: 2070 us
  other arithmetic  474 us (23%)
  local copies, waits for them, and re-layouts  458 us (22%)
  waiting for transfers between devices  421 us (20%)
  blocking collectives  367 us (18%)
  matrix products  324 us (16%)
    unnamed x8, other arithmetic  394 us
    psum x2, waiting for transfers between devices, per_device(): barycenter = jnp.exp(lax.psum(value_portion, 'img') / total_weight)  328 us
    all_to_all x4, blocking collectives, apply_kernel(): lax.all_to_all(inner, 'slab', split_axis=2, concat_axis=1, tiled=True)  236 us
    unnamed x60, local copies, waits for them, and re-layouts  174 us
    dot_general x20, matrix products, rows_pass(): lax.dot_general(terms[:, offset], split[offset:offset + block_stack], (((...  165 us
    dot_general x20, matrix products, column_sweep(): lax.dot_general(padded[offset:offset + block_stack], terms[:, offset], ((...  160 us
    all_to_all x2, blocking collectives, apply_kernel(): lax.all_to_all(result, 'slab', split_axis=1, concat_axis=2, tiled=True)  114 us
    all_to_all x2, waiting for transfers between devices, apply_kernel(): lax.all_to_all(result, 'slab', split_axis=1, concat_axis=2, tiled=True)  93.1 us
  transfers between devices with their start and end apart: 4, of which 4 were waited for; matrix products, arithmetic and copies ran while one was open for 3% of the time, Pallas kernels for 0%

commit v1 on v0

--- a/solution.py
+++ b/solution.py
@@ -58,7 +58,12 @@
 
     def apply_kernel(field):
         inner = column_sweep(field, terms).astype(jnp.bfloat16)
-        columns = lax.all_to_all(inner, "slab", split_axis=2, concat_axis=1, tiled=True)
+        columns = jnp.concatenate(
+            lax.all_to_all(
+                jnp.stack(jnp.split(inner, lax.axis_size("slab"), axis=2)), "slab", 0, 0
+            ),
+            axis=1,
+        )
         padded = jnp.pad(columns, ((0, 0), (2 * width, 2 * width), (0, 0)))
         result = rows_pass(padded, terms).astype(jnp.bfloat16)
         return lax.all_to_all(result, "slab", split_axis=1, concat_axis=2, tiled=True)

time: 2080 us -> 1770 us (0.85)
  other arithmetic: 474 us -> 284 us
  local copies, waits for them, and re-layouts: 458 us -> 351 us
    unnamed x8 -> x4, other arithmetic: 394 us -> 196 us
    unnamed x60 -> x56, local copies, waits for them, and re-layouts: 174 us -> 116 us
    convert_element_type x4 -> x0, local copies, waits for them, and re-layouts: 38.6 us -> none  [apply_kernel(): inner = column_sweep(field, terms).astype(jnp.bfloat16)]
    all_to_all x4 -> x0, local copies, waits for them, and re-layouts: 26.4 us -> none  [apply_kernel(): lax.all_to_all(inner, 'slab', split_axis=2, concat_axis=1, tiled=True)]
where the time goes in v1:
time: 1770 us; the launch traced here: 1750 us
  waiting for transfers between devices  419 us (24%)
  blocking collectives  357 us (20%)
  local copies, waits for them, and re-layouts  351 us (20%)
  matrix products  314 us (18%)
  other arithmetic  284 us (16%)
    psum x2, waiting for transfers between devices, per_device(): barycenter = jnp.exp(lax.psum(value_portion, 'img') / total_weight)  326 us
    all_to_all x4, blocking collectives, apply_kernel(): lax.all_to_all(jnp.stack(jnp.split(inner, lax.axis_size('slab'), axis=2))...  226 us
    unnamed x4, other arithmetic  196 us
    dot_general x20, matrix products, column_sweep(): lax.dot_general(padded[offset:offset + block_stack], terms[:, offset], ((...  160 us
    dot_general x20, matrix products, rows_pass(): lax.dot_general(terms[:, offset], split[offset:offset + block_stack], (((...  154 us
    unnamed x56, local copies, waits for them, and re-layouts  116 us
    all_to_all x2, blocking collectives, apply_kernel(): lax.all_to_all(result, 'slab', split_axis=1, concat_axis=2, tiled=True)  113 us
    all_to_all x2, waiting for transfers between devices, apply_kernel(): lax.all_to_all(result, 'slab', split_axis=1, concat_axis=2, tiled=True)  92.5 us
  transfers between devices with their start and end apart: 4, of which 4 were waited for; matrix products, arithmetic and copies ran while one was open for 3% of the time, Pallas kernels for 0%

profile of v1, /device:TPU:0, one launch (start us, length us, event | category | flops | bytes accessed | tf_op | source)
XLA Modules:
  0.0 1749.9 jit_solution(4947922025691061084)
XLA Ops:
  79.1 59.0 %all_to_all.56 = bf16[4,1,768,768]{3,2,1,0:T(8,128)(2,1)S(1)} all-to-all(bf16[4,1,768,768]{3,2,1,0:T(8,128)(2,1)S(1)} %pad_maximum_fusion), channel_id=1, replica_groups=mesh['img'=8,'slab'=4] {'slab'}, dimensions={0} | all-to-all | bytes 9437184 | tf_op jit(solution)/shard_map/all_to_all | solution.py:62
  161.8 18.2 %add_convert_fusion.6 = bf16[24,128,768]{2,1,0:T(8,128)(2,1)} fusion(f32[24,128,768]{2,1,0:T(8,128)} %fusion.67, f32[24,128,768]{2,1,0:T(8,128)} %fusion.63, f32[24,128,768]{2,1,0:T(8,128)} %fusion.55, f32[24,128,768]{2,1,0:T(8,128)} %fusion.59, bf16[24,128,768]{2,1,0:T(8,128)(2,1)} %bitcast.288, bf16[24,5,128,128]{3,2,1,0:T(8,128)(2,1)} %copy-done), kind=kOutput, calls=%fused_computation.21 | convolution fusion | flops 615776256 | bytes 47972352 | tf_op jit(solution)/shard_map/dot_general | solution.py:43
  190.0 49.0 %reduce.1 = bf16[3072,768]{1,0:T(8,128)(2,1)} reduce(bf16[3072,1,768]{2,1,0:T(2,128)(2,1)} %bitcast.275, bf16[]{:T(256)} %broadcast.49), dimensions={1}, to_apply=%bitcast.261.reduce_sub_computation | reduce | bytes 9437186
  259.2 42.2 %all-to-all-done.1 = bf16[4,2,294912]{2,1,0:T(2,128)(2,1)} async-done(((bf16[4,2,294912]{2,1,0:T(2,128)(2,1)}), bf16[4,2,294912]{2,1,0:T(2,128)(2,1)}, u32[]{:S(2)}, u32[]{:S(2)}) %all-to-all-start.1) | async-done | bytes 4718624 | tf_op jit(solution)/shard_map/all_to_all | solution.py:69
  309.4 23.6 %copy.99 = f32[1,4,768,768]{2,3,1,0:T(8,128)} copy(bf16[1,4,768,768]{3,0,2,1:T(2,128)(2,1)} %bitcast.277) | data formatting | bytes 14155776 | tf_op jit(solution)/shard_map/convert_element_type | solution.py:75
  401.3 56.2 %all_to_all.57 = bf16[4,1,768,768]{3,2,1,0:T(8,128)(2,1)S(1)} all-to-all(bf16[4,1,768,768]{3,2,1,0:T(8,128)(2,1)S(1)} %pad_maximum_fusion.1), channel_id=1, replica_groups=mesh['img'=8,'slab'=4] {'slab'}, dimensions={0} | all-to-all | bytes 9437184 | tf_op jit(solution)/shard_map/all_to_all | solution.py:62
  481.1 18.2 %add_convert_fusion.4 = bf16[24,128,768]{2,1,0:T(8,128)(2,1)} fusion(f32[24,128,768]{2,1,0:T(8,128)} %fusion.66, f32[24,128,768]{2,1,0:T(8,128)} %fusion.62, f32[24,128,768]{2,1,0:T(8,128)} %fusion.54, f32[24,128,768]{2,1,0:T(8,128)} %fusion.58, bf16[24,128,768]{2,1,0:T(8,128)(2,1)} %bitcast.289, bf16[24,5,128,128]{3,2,1,0:T(8,128)(2,1)} %copy-done), kind=kOutput, calls=%fused_computation.19 | convolution fusion | flops 615776256 | bytes 47972352 | tf_op jit(solution)/shard_map/dot_general | solution.py:43
  508.8 49.1 %reduce.2 = bf16[3072,768]{1,0:T(8,128)(2,1)} reduce(bf16[3072,1,768]{2,1,0:T(2,128)(2,1)} %bitcast.278, bf16[]{:T(256)} %broadcast.49), dimensions={1}, to_apply=%bitcast.260.reduce_sub_computation | reduce | bytes 9437186
  569.0 50.3 %all-to-all-done.3 = bf16[4,2,294912]{2,1,0:T(2,128)(2,1)} async-done(((bf16[4,2,294912]{2,1,0:T(2,128)(2,1)}), bf16[4,2,294912]{2,1,0:T(2,128)(2,1)}, u32[]{:S(2)}, u32[]{:S(2)}) %all-to-all-start.3) | async-done | bytes 4718624 | tf_op jit(solution)/shard_map/all_to_all | solution.py:69
  642.7 23.3 %copy.107 = f32[1,4,768,768]{2,3,1,0:T(8,128)} copy(f32[1,4,768,768]{3,0,2,1:T(1,128)} %bitcast.282) | data formatting | bytes 18874368 | tf_op jit(solution)/shard_map/i,irc->rc/dot_general | solution.py:77
  683.4 23.6 %copy.108 = f32[1,4,768,768]{2,3,1,0:T(8,128)} copy(bf16[1,4,768,768]{3,0,2,1:T(2,128)(2,1)} %bitcast.262) | data formatting | bytes 14155776 | tf_op jit(solution)/shard_map/convert_element_type | solution.py:77
  707.0 155.0 %all-reduce.11.cloned.1.call-done = f32[768,3072]{0,1:T(8,128)} async-done(((f32[768,3072]{0,1:T(8,128)}), f32[768,3072]{0,1:T(8,128)}) %all-reduce.11.cloned.1.call-update) | async-done | bytes 9437200 | tf_op jit(solution)/shard_map/psum | solution.py:78
  930.8 57.4 %all_to_all.58 = bf16[4,1,768,768]{3,2,1,0:T(8,128)(2,1)S(1)} all-to-all(bf16[4,1,768,768]{3,2,1,0:T(8,128)(2,1)S(1)} %pad_maximum_fusion.2), channel_id=1, replica_groups=mesh['img'=8,'slab'=4] {'slab'}, dimensions={0} | all-to-all | bytes 9437184 | tf_op jit(solution)/shard_map/all_to_all | solution.py:62
  1011.8 18.2 %add_convert_fusion.2 = bf16[24,128,768]{2,1,0:T(8,128)(2,1)} fusion(f32[24,128,768]{2,1,0:T(8,128)} %fusion.65, f32[24,128,768]{2,1,0:T(8,128)} %fusion.61, f32[24,128,768]{2,1,0:T(8,128)} %fusion.53, f32[24,128,768]{2,1,0:T(8,128)} %fusion.57, bf16[24,128,768]{2,1,0:T(8,128)(2,1)} %bitcast.290, bf16[24,5,128,128]{3,2,1,0:T(8,128)(2,1)} %copy-done), kind=kOutput, calls=%fused_computation.16 | convolution fusion | flops 615776256 | bytes 47972352 | tf_op jit(solution)/shard_map/dot_general | solution.py:43
  1039.5 49.1 %reduce.3 = bf16[3072,768]{1,0:T(8,128)(2,1)} reduce(bf16[3072,1,768]{2,1,0:T(2,128)(2,1)} %bitcast.279, bf16[]{:T(256)} %broadcast.49), dimensions={1}, to_apply=%bitcast.259.reduce_sub_computation | reduce | bytes 9437186
  1093.9 58.0 %all_to_all.59 = bf16[4,2,294912]{2,1,0:T(2,128)(2,1)} all-to-all(bf16[4,2,294912]{2,1,0:T(2,128)(2,1)} %reshape.264), channel_id=1, replica_groups=mesh['img'=8,'slab'=4] {'slab'}, dimensions={0} | all-to-all | bytes 9437184 | tf_op jit(solution)/shard_map/all_to_all | solution.py:69
  1160.0 23.6 %copy.115 = f32[1,4,768,768]{2,3,1,0:T(8,128)} copy(bf16[1,4,768,768]{3,0,2,1:T(2,128)(2,1)} %bitcast.280) | data formatting | bytes 14155776 | tf_op jit(solution)/shard_map/convert_element_type | solution.py:75
  1251.9 53.8 %all_to_all.60 = bf16[4,1,768,768]{3,2,1,0:T(8,128)(2,1)S(1)} all-to-all(bf16[4,1,768,768]{3,2,1,0:T(8,128)(2,1)S(1)} %pad_maximum_fusion.3), channel_id=1, replica_groups=mesh['img'=8,'slab'=4] {'slab'}, dimensions={0} | all-to-all | bytes 9437184 | tf_op jit(solution)/shard_map/all_to_all | solution.py:62
  1329.3 18.2 %add_convert_fusion = bf16[24,128,768]{2,1,0:T(8,128)(2,1)} fusion(f32[24,128,768]{2,1,0:T(8,128)} %fusion.64, f32[24,128,768]{2,1,0:T(8,128)} %fusion.60, f32[24,128,768]{2,1,0:T(8,128)} %fusion.52, f32[24,128,768]{2,1,0:T(8,128)} %fusion.56, bf16[24,128,768]{2,1,0:T(8,128)(2,1)} %bitcast.287, bf16[24,5,128,128]{3,2,1,0:T(8,128)(2,1)} %copy-done), kind=kOutput, calls=%fused_computation.14 | convolution fusion | flops 615776256 | bytes 47972352 | tf_op jit(solution)/shard_map/dot_general | solution.py:43
  1357.0 49.2 %reduce.4 = bf16[3072,768]{1,0:T(8,128)(2,1)} reduce(bf16[3072,1,768]{2,1,0:T(2,128)(2,1)} %bitcast.276, bf16[]{:T(256)} %broadcast.49), dimensions={1}, to_apply=%bitcast.258.reduce_sub_computation | reduce | bytes 9437186
  1411.6 55.5 %all_to_all.61 = bf16[4,2,294912]{2,1,0:T(2,128)(2,1)} all-to-all(bf16[4,2,294912]{2,1,0:T(2,128)(2,1)} %reshape.266), channel_id=1, replica_groups=mesh['img'=8,'slab'=4] {'slab'}, dimensions={0} | all-to-all | bytes 9437184 | tf_op jit(solution)/shard_map/all_to_all | solution.py:69
  1490.4 23.2 %copy.123 = f32[1,4,768,768]{2,3,1,0:T(8,128)} copy(f32[1,4,768,768]{3,0,2,1:T(1,128)} %bitcast.281) | data formatting | bytes 18874368 | tf_op jit(solution)/shard_map/i,irc->rc/dot_general | solution.py:77
  1513.7 23.4 %copy.124 = f32[1,4,768,768]{2,3,1,0:T(8,128)} copy(bf16[1,4,768,768]{3,0,2,1:T(2,128)(2,1)} %bitcast.263) | data formatting | bytes 14155776 | tf_op jit(solution)/shard_map/convert_element_type | solution.py:77
  1537.1 171.2 %all-reduce.13.cloned.1.call-done = f32[768,3072]{0,1:T(8,128)} async-done(((f32[768,3072]{0,1:T(8,128)}), f32[768,3072]{0,1:T(8,128)}) %all-reduce.13.cloned.1.call-update) | async-done | bytes 9437200 | tf_op jit(solution)/shard_map/psum | solution.py:78
  (128 shorter events, 566.0 us)
Async XLA Ops:
  15.6 6.9 copy-start.12
  26.3 18.9 %copy-start = (bf16[24,5,128,128]{3,2,1,0:T(8,128)(2,1)}, bf16[24,5,128,128]{3,2,1,0:T(8,128)(2,1)S(1)}, u32[]{:S(2)}) copy-start(bf16[24,5,128,128]{3,2,1,0:T(8,128)(2,1)S(1)} %select_reduce_fusion) | copy-start | bytes 11796484
  26.3 8.9 copy-start.8
  79.1 59.0 %copy-start.1 = (bf16[24,5,128,128]{3,2,1,0:T(8,128)(2,1)S(1)}, bf16[24,5,128,128]{3,2,1,0:T(8,128)(2,1)}, u32[]{:S(2)}) copy-start(bf16[24,5,128,128]{3,2,1,0:T(8,128)(2,1)} %copy-done) | copy-start | bytes 11796484
  244.5 56.9 %all-to-all-start.1 = ((bf16[4,2,294912]{2,1,0:T(2,128)(2,1)}), bf16[4,2,294912]{2,1,0:T(2,128)(2,1)}, u32[]{:S(2)}, u32[]{:S(2)}) async-start(bf16[4,2,294912]{2,1,0:T(2,128)(2,1)} %reshape.260), calls=%async_computation.1 | async-start | bytes 9437184 | tf_op jit(solution)/shard_map/all_to_all | solution.py:69
  349.6 7.7 copy-start.2
  349.6 7.7 copy-start.9
  401.3 56.2 %copy-start.3 = (bf16[24,5,128,128]{3,2,1,0:T(8,128)(2,1)S(1)}, bf16[24,5,128,128]{3,2,1,0:T(8,128)(2,1)}, u32[]{:S(2)}) copy-start(bf16[24,5,128,128]{3,2,1,0:T(8,128)(2,1)} %copy-done) | copy-start | bytes 11796484
  563.3 56.0 %all-to-all-start.3 = ((bf16[4,2,294912]{2,1,0:T(2,128)(2,1)}), bf16[4,2,294912]{2,1,0:T(2,128)(2,1)}, u32[]{:S(2)}, u32[]{:S(2)}) async-start(bf16[4,2,294912]{2,1,0:T(2,128)(2,1)} %reshape.262), calls=%async_computation.3 | async-start | bytes 9437184 | tf_op jit(solution)/shard_map/all_to_all | solution.py:69
  568.3 293.7 %all-reduce.11.cloned.1.call-start = ((), (), s32[]{:S(2)}) async-start(), calls=%async_computation.8 | async-start | bytes 18874368 | tf_op jit(solution)/shard_map/psum | solution.py:78
  666.1 1042.3 %all-reduce.13.cloned.1.call-start = ((), (), s32[]{:S(2)}) async-start(), calls=%async_computation.9 | async-start | bytes 18874368 | tf_op jit(solution)/shard_map/psum | solution.py:78
  879.1 7.7 copy-start.4
  879.1 7.7 copy-start.10
  930.8 57.4 %copy-start.5 = (bf16[24,5,128,128]{3,2,1,0:T(8,128)(2,1)S(1)}, bf16[24,5,128,128]{3,2,1,0:T(8,128)(2,1)}, u32[]{:S(2)}) copy-start(bf16[24,5,128,128]{3,2,1,0:T(8,128)(2,1)} %copy-done) | copy-start | bytes 11796484
  1200.2 7.8 copy-start.6
  1200.2 7.8 copy-start.11
  1251.9 53.8 %copy-start.7 = (bf16[24,5,128,128]{3,2,1,0:T(8,128)(2,1)S(1)}, bf16[24,5,128,128]{3,2,1,0:T(8,128)(2,1)}, u32[]{:S(2)}) copy-start(bf16[24,5,128,128]{3,2,1,0:T(8,128)(2,1)} %copy-done) | copy-start | bytes 11796484
Sparse Core Ops, SparseCore 0:
  666.2 195.7 all-reduce.10
  1513.8 194.4 all-reduce.12
